TPU v7x, 256 devices: a whole 4x4x8 slice. The times are simulated.
256 devices in a mesh: fsdp: 64 (over x_lo, z, y), dp: 4 (over x_hi, core).
Axes of the slice: x: 4 (x_hi: 2, x_lo: 2; x = x_hi * 2 + x_lo), y: 4, z: 8, core: 2. Of those that a mesh axis runs over, the one named last changes fastest.
Arguments:
- tokens: bfloat16 [4, 8192, 8192], P('dp', 'fsdp'), may hold values from -6 to 6
- queries: bfloat16 [4, 8192, 4096], P('dp', 'fsdp'), may hold values from -40 to 40, as said below
- keys: bfloat16 [4, 8192, 512], P('dp', 'fsdp'), may hold values from -4 to 4
- memory: bfloat16 [4, 8192, 8192], P('dp', 'fsdp'), may hold values from -6 to 6
- mem_keys: bfloat16 [4, 8192, 512], P('dp', 'fsdp'), may hold values from -4 to 4
- cotangent: bfloat16 [4, 8192, 4096], P('dp', 'fsdp'), may hold values from -6 to 6
- value_weight: bfloat16 [8192, 512], P('fsdp'), may hold values from -0.0625 to 0.0625
- dest_group: int32 [4, 128], P('dp', 'fsdp'), may hold values from 0 to 3, as said below
- source_group: int32 [4, 128], P('dp', 'fsdp'), may hold values from 0 to 3, as said below
- lengths: int32 [4, 128], P('dp', 'fsdp'), may hold values from 1 to 64
Outputs:
- grad_queries: bfloat16 [4, 8192, 4096], P('dp', 'fsdp')
- grad_keys: bfloat16 [4, 8192, 512], P('dp', 'fsdp')
- grad_memory: bfloat16 [4, 8192, 8192], P('dp', 'fsdp')
- grad_mem_keys: bfloat16 [4, 8192, 512], P('dp', 'fsdp')
- grad_weight: bfloat16 [8192, 512], P('fsdp')
Inputs may be any that keep to these rules, and one draw needn't show every extreme that they name: `queries`: large in the hidden draw where a query row copies its own key. `dest_group`: the 2 documents of a device go to two different groups, never its own; document k of every device of one fsdp index moves the same number of groups ahead. `source_group`: consistent with dest_group: every device receives exactly one document for each of its slots, at most one from each sender.
All inputs are finite; a program needn't handle non-finite values.
Results may differ from a plain program's by a relative error of at most 0.0075.
Values may be sent and summed in bfloat16 or wider, within the bound.
No kernel may reach another device: no remote copies, remote signals or barrier semaphores. Data moves between devices by JAX's collectives and lax.ppermute only.
A program may use at most 128 MiB of HBM per device.

v0:
```python
import jax
import jax.numpy as jnp
from jax import lax
from jax.sharding import Mesh, PartitionSpec as P

HEAD_DIM = 128


def attend(query_rows, seg_keys, seg_values, slot_keys, slot_values, upstream, length):
    seg_len = query_rows.shape[0]
    mem_len = slot_keys.shape[0]
    kv_width = seg_keys.shape[1]
    heads_kv = kv_width // HEAD_DIM
    group_size = query_rows.shape[1] // kv_width
    key_count = seg_len + mem_len
    all_keys = jnp.concatenate([slot_keys, seg_keys], axis=0).reshape(key_count, heads_kv, HEAD_DIM)
    all_values = jnp.concatenate([slot_values, seg_values], axis=0).reshape(
        key_count, heads_kv, HEAD_DIM
    )
    query_heads = query_rows.reshape(seg_len, heads_kv, group_size, HEAD_DIM)
    score_scale = HEAD_DIM ** (-0.5)
    scores = (
        jnp.einsum("qkgd,jkd->kgqj", query_heads, all_keys, preferred_element_type=jnp.float32)
        * score_scale
    )
    positions = jnp.arange(seg_len)[:, None]
    columns = jnp.arange(key_count)[None, :]
    visible = (columns < mem_len) | (columns - mem_len <= positions)
    scores = jnp.where(visible, scores, -1e30)
    row_max = jnp.max(scores, axis=-1, keepdims=True)
    exp_scores = jnp.exp(scores - row_max)
    weights = exp_scores / jnp.sum(exp_scores, axis=-1, keepdims=True)
    weights_low = weights.astype(jnp.bfloat16)
    output = jnp.einsum(
        "kgqj,jkd->qkgd", weights_low, all_values, preferred_element_type=jnp.float32
    ).astype(jnp.bfloat16)
    live_rows = (jnp.arange(seg_len) < length).astype(jnp.bfloat16)
    masked = (
        upstream.reshape(seg_len, heads_kv, group_size, HEAD_DIM) * live_rows[:, None, None, None]
    )
    grad_weights = jnp.einsum(
        "qkgd,jkd->kgqj", masked, all_values, preferred_element_type=jnp.float32
    )
    grad_values = jnp.einsum(
        "kgqj,qkgd->jkd", weights_low, masked, preferred_element_type=jnp.float32
    ).reshape(key_count, kv_width)
    row_delta = jnp.einsum("qkgd,qkgd->kgq", masked, output, preferred_element_type=jnp.float32)
    grad_scores = (weights * (grad_weights - row_delta[..., None]) * score_scale).astype(
        jnp.bfloat16
    )
    grad_query = (
        jnp.einsum("kgqj,jkd->qkgd", grad_scores, all_keys, preferred_element_type=jnp.float32)
        .reshape(seg_len, -1)
        .astype(jnp.bfloat16)
    )
    grad_all_keys = jnp.einsum(
        "kgqj,qkgd->jkd", grad_scores, query_heads, preferred_element_type=jnp.float32
    ).reshape(key_count, kv_width)
    return (
        grad_query,
        grad_all_keys[:mem_len],
        grad_all_keys[mem_len:],
        grad_values[:mem_len],
        grad_values[mem_len:],
    )


FSDP_AXES = ("fx", "fz", "fy")
DP_AXES = ("dx", "dc")


def to_block_order(cols, split):
    fx, fz, fy = split
    rows = cols.shape[0]
    block = cols.shape[1] // (fx * fz * fy)
    return cols.reshape(rows, fx, fz, fy, block).transpose(0, 2, 3, 1, 4).reshape(rows, -1)


def from_block_order(cols, split):
    fx, fz, fy = split
    rows = cols.shape[0]
    block = cols.shape[1] // (fx * fz * fy)
    return cols.reshape(rows, fz, fy, fx, block).transpose(0, 3, 1, 2, 4).reshape(rows, -1)


def per_device(
    tokens,
    queries,
    keys,
    memory,
    mem_keys,
    cotangent,
    value_weight,
    dest_group,
    source_group,
    lengths,
):
    split = tuple((lax.axis_size(a) for a in FSDP_AXES))
    cores = lax.axis_size("dc")
    groups = lax.axis_size("dx") * cores
    slot_count = dest_group.shape[1]
    seg_len = tokens.shape[1] // slot_count
    mem_len = memory.shape[1] // slot_count
    kv_width = value_weight.shape[1]
    model_width = tokens.shape[2]
    half = kv_width // cores
    core = lax.axis_index("dc")
    part = lax.dynamic_slice_in_dim(value_weight, core * half, half, axis=1)
    part = lax.all_gather(part, "fx", axis=0, tiled=True)
    part = lax.all_gather(part, "fy", axis=0, tiled=True)
    part = lax.all_gather(part, "fz", axis=0, tiled=True)
    weight_full = lax.all_gather(part, "dc", axis=1, tiled=True)
    stacked = to_block_order(jnp.concatenate([tokens[0], memory[0]], axis=0), split)
    partner_stacked = lax.ppermute(stacked, "dc", [(c, (c + 1) % cores) for c in range(cores)])
    values = jnp.dot(stacked, weight_full, preferred_element_type=jnp.float32).astype(jnp.bfloat16)
    split_at = slot_count * seg_len
    seg_values = values[:split_at].reshape(slot_count, seg_len, kv_width)
    doc_values = values[split_at:].reshape(slot_count, mem_len, kv_width)
    doc_keys = mem_keys[0].reshape(slot_count, mem_len, kv_width)
    targets = jnp.arange(groups, dtype=jnp.int32)
    send_table = (dest_group[0][None, :] == targets[:, None]).astype(jnp.bfloat16)
    take_table = (source_group[0][:, None] == targets[None, :]).astype(jnp.bfloat16)
    out_keys = jnp.einsum(
        "hs,smc->hmc", send_table, doc_keys, preferred_element_type=jnp.float32
    ).astype(jnp.bfloat16)
    out_values = jnp.einsum(
        "hs,smc->hmc", send_table, doc_values, preferred_element_type=jnp.float32
    ).astype(jnp.bfloat16)
    in_keys, in_values = (
        lax.all_to_all(out_keys, DP_AXES, split_axis=0, concat_axis=0, tiled=True),
        lax.all_to_all(out_values, DP_AXES, split_axis=0, concat_axis=0, tiled=True),
    )
    slot_keys = jnp.einsum(
        "sh,hmc->smc", take_table, in_keys, preferred_element_type=jnp.float32
    ).astype(jnp.bfloat16)
    slot_values = jnp.einsum(
        "sh,hmc->smc", take_table, in_values, preferred_element_type=jnp.float32
    ).astype(jnp.bfloat16)
    query_slots = queries[0].reshape(slot_count, seg_len, -1)
    key_slots = keys[0].reshape(slot_count, seg_len, kv_width)
    upstream_slots = cotangent[0].reshape(slot_count, seg_len, -1)
    grad_query, slot_grad_keys, seg_grad_keys, slot_grad_values, seg_grad_values = jax.vmap(attend)(
        query_slots, key_slots, seg_values, slot_keys, slot_values, upstream_slots, lengths[0]
    )
    back_keys = jnp.einsum(
        "sh,smc->hmc",
        take_table,
        slot_grad_keys.astype(jnp.bfloat16),
        preferred_element_type=jnp.float32,
    ).astype(jnp.bfloat16)
    back_values = jnp.einsum(
        "sh,smc->hmc",
        take_table,
        slot_grad_values.astype(jnp.bfloat16),
        preferred_element_type=jnp.float32,
    ).astype(jnp.bfloat16)
    ret_keys, ret_values = (
        lax.all_to_all(back_keys, DP_AXES, split_axis=0, concat_axis=0, tiled=True),
        lax.all_to_all(back_values, DP_AXES, split_axis=0, concat_axis=0, tiled=True),
    )
    doc_grad_keys = jnp.einsum(
        "hs,hmc->smc", send_table, ret_keys, preferred_element_type=jnp.float32
    ).astype(jnp.bfloat16)
    doc_grad_values = jnp.einsum(
        "hs,hmc->smc", send_table, ret_values, preferred_element_type=jnp.float32
    ).astype(jnp.bfloat16)
    doc_grad_flat = doc_grad_values.reshape(slot_count * mem_len, kv_width)
    grad_memory = from_block_order(
        lax.dot_general(
            doc_grad_flat, weight_full, (((1,), (1,)), ((), ())), preferred_element_type=jnp.float32
        ).astype(jnp.bfloat16),
        split,
    )
    value_grads_all = jnp.concatenate(
        [seg_grad_values.astype(jnp.bfloat16).reshape(-1, kv_width), doc_grad_flat], axis=0
    )
    grads_half = lax.dynamic_slice_in_dim(value_grads_all, core * half, half, axis=1)
    swap = [(c, (c + 1) % cores) for c in range(cores)]
    partner_grads = lax.ppermute(
        lax.dynamic_slice_in_dim(value_grads_all, (1 - core) * half, half, axis=1), "dc", swap
    )
    both_rows = jnp.concatenate([stacked, partner_stacked], axis=0)
    both_grads = jnp.concatenate([grads_half, partner_grads], axis=0)
    partial = lax.dot_general(
        both_rows, both_grads, (((0,), (0,)), ((), ())), preferred_element_type=jnp.float32
    )
    quarter = half // 2
    fx, fz, fy = split
    first = partial[:, :quarter]
    second = partial[:, quarter:].reshape(fz, fy, fx, -1, quarter).transpose(1, 0, 2, 3, 4)
    second = second.reshape(-1, quarter)
    first = lax.psum_scatter(first, "fz", scatter_dimension=0, tiled=True)
    second = lax.psum_scatter(second, "fy", scatter_dimension=0, tiled=True)
    first = lax.psum_scatter(first, "fy", scatter_dimension=0, tiled=True)
    second = lax.psum_scatter(second, "fz", scatter_dimension=0, tiled=True)
    first = lax.psum_scatter(first, "fx", scatter_dimension=0, tiled=True)
    second = lax.psum_scatter(second, "fx", scatter_dimension=0, tiled=True)
    shares = lax.psum(jnp.concatenate([first, second], axis=1), "dx")
    grad_weight = lax.all_gather(shares, "dc", axis=1, tiled=True).astype(jnp.bfloat16)
    return (
        grad_query.reshape(1, slot_count * seg_len, -1),
        seg_grad_keys.astype(jnp.bfloat16).reshape(1, slot_count * seg_len, kv_width),
        grad_memory.reshape(1, slot_count * mem_len, model_width),
        doc_grad_keys.reshape(1, slot_count * mem_len, kv_width),
        grad_weight,
    )


def refined_mesh(mesh):
    fsdp, dp = (mesh.shape["fsdp"], mesh.shape["dp"])
    devices = mesh.devices.reshape(2, fsdp // 2 // 4, 4, 2, dp // 2)
    return Mesh(devices, FSDP_AXES + DP_AXES)


def solution(mesh):
    fine = refined_mesh(mesh)
    row = P(DP_AXES, FSDP_AXES, None)
    table = P(DP_AXES, FSDP_AXES)
    in_specs = (row, row, row, row, row, row, P(FSDP_AXES, None), table, table, table)
    out_specs = (row, row, row, row, P(FSDP_AXES, None))
    return jax.shard_map(
        per_device, mesh=fine, in_specs=in_specs, out_specs=out_specs, check_vma=False
    )
```

profile of v0, /device:TPU:1, one launch (start us, length us, event | category | flops | bytes accessed | tf_op | source)
XLA Modules:
  0.0 414.3 jit_solution(141352072827042103)
XLA Ops:
  10.4 4.1 copy.66
  23.4 4.0 all-to-all-start
  28.3 5.8 %all-to-all-done = bf16[4,64,512]{2,1,0:T(8,128)(2,1)} async-done(((bf16[4,64,512]{2,1,0:T(8,128)(2,1)}), bf16[4,64,512]{2,1,0:T(8,128)(2,1)}, u32[]{:S(2)}, u32[]{:S(2)}) %all-to-all-start) | async-done | bytes 262176 | tf_op jit(solution)/shard_map/all_to_all | solution.py:130
  42.1 4.3 %all-to-all-start.2 = ((bf16[4,64,512]{2,1,0:T(8,128)(2,1)}), bf16[4,64,512]{2,1,0:T(8,128)(2,1)S(1)}, u32[]{:S(2)}, u32[]{:S(2)}) async-start(bf16[4,64,512]{2,1,0:T(8,128)(2,1)} %copy.78), calls=%async_computation.2 | async-start | bytes 524288 | tf_op jit(solution)/shard_map/all_to_all | solution.py:159
  46.6 6.4 %all-to-all-done.2 = bf16[4,64,512]{2,1,0:T(8,128)(2,1)S(1)} async-done(((bf16[4,64,512]{2,1,0:T(8,128)(2,1)}), bf16[4,64,512]{2,1,0:T(8,128)(2,1)S(1)}, u32[]{:S(2)}, u32[]{:S(2)}) %all-to-all-start.2) | async-done | bytes 262176 | tf_op jit(solution)/shard_map/all_to_all | solution.py:159
  55.5 4.8 %fusion.2 = f32[8192,256]{1,0:T(8,128)S(1)} fusion(bf16[256,8192]{0,1:T(8,128)(2,1)} %collective-permute-done, bf16[256,8192]{0,1:T(8,128)(2,1)} %bitcast.14, bf16[256,256]{1,0:T(8,128)(2,1)S(1)} %collective-permute-done.1, bf16[256,256]{1,0:T(8,128)(2,1)S(1)} %get-tuple-element.7), kind=kOutput, calls=%fused_computation.3 | convolution fusion | flops 2164785152 | bytes 17039360 | tf_op jit(solution)/shard_map/dot_general | solution.py:184
  60.3 3.9 fusion.68
  64.2 4.6 %copy.87 = f32[4,8,2,128,128]{4,3,2,1,0:T(8,128)} copy(f32[4,8,2,128,128]{4,3,2,0,1:T(8,128)} %bitcast.138) | data formatting | bytes 8388608 | tf_op jit(solution)/shard_map/transpose | solution.py:190
  68.9 50.1 %reduce-scatter.7.cloned.1.call-done = f32[1024,128]{1,0:T(8,128)} async-done(((f32[8192,128]{1,0:T(8,128)}), f32[1024,128]{1,0:T(8,128)}) %reduce-scatter.7.cloned.1.call-update) | async-done | bytes 524304 | tf_op jit(solution)/shard_map/reduce_scatter | solution.py:192
  119.1 50.6 %reduce-scatter.13.cloned.1.call-done = f32[2048,128]{1,0:T(8,128)} async-done(((f32[8192,128]{1,0:T(8,128)}), f32[2048,128]{1,0:T(8,128)}) %reduce-scatter.13.cloned.1.call-update) | async-done | bytes 1048592 | tf_op jit(solution)/shard_map/reduce_scatter | solution.py:193
  173.5 11.0 %all_gather.16 = bf16[1024,256]{1,0:T(8,128)(2,1)} all-gather(bf16[256,256]{1,0:T(8,128)(2,1)S(1)} %all_gather.15), channel_id=1, replica_groups=mesh['fx'=2,'fz'=8,'fy'=4,'dx'=2,'dc'=2] {'fy'}, dimensions={0}, use_global_device_ids=true | all-gather | bytes 655360 | tf_op jit(solution)/shard_map/all_gather | solution.py:110
  184.6 9.3 %reduce-scatter.9.cloned.1.call-done = f32[256,128]{1,0:T(8,128)} async-done(((f32[1024,128]{1,0:T(8,128)}), f32[256,128]{1,0:T(8,128)}) %reduce-scatter.9.cloned.1.call-update) | async-done | bytes 131088 | tf_op jit(solution)/shard_map/reduce_scatter | solution.py:194
  193.9 38.3 %reduce-scatter.15.cloned.1.call-done = f32[256,128]{1,0:T(8,128)} async-done(((f32[2048,128]{1,0:T(8,128)}), f32[256,128]{1,0:T(8,128)}) %reduce-scatter.15.cloned.1.call-update) | async-done | bytes 131088 | tf_op jit(solution)/shard_map/reduce_scatter | solution.py:195
  232.3 59.8 %all-gather.3.cloned.1.call-done = bf16[8192,256]{1,0:T(8,128)(2,1)} async-done(((bf16[1024,256]{1,0:T(8,128)(2,1)}), bf16[8192,256]{1,0:T(8,128)(2,1)}) %all-gather.3.cloned.1.call-update) | async-done | bytes 4194320 | tf_op jit(solution)/shard_map/all_gather | solution.py:111
  292.2 16.3 %reduce-scatter.11.cloned.1.call-done = f32[128,128]{1,0:T(8,128)} async-done(((f32[256,128]{1,0:T(8,128)}), f32[128,128]{1,0:T(8,128)}) %reduce-scatter.11.cloned.1.call-update) | async-done | bytes 65552 | tf_op jit(solution)/shard_map/reduce_scatter | solution.py:196
  308.5 18.9 %reduce-scatter.17.cloned.1.call-done = f32[128,128]{1,0:T(8,128)} async-done(((f32[256,128]{1,0:T(8,128)}), f32[128,128]{1,0:T(8,128)}) %reduce-scatter.17.cloned.1.call-update) | async-done | bytes 65552 | tf_op jit(solution)/shard_map/reduce_scatter | solution.py:197
  328.3 10.4 %all-reduce.1 = bf16[128,256]{1,0:T(8,128)(2,1)S(1)} all-reduce(f32[128,256]{1,0:T(8,128)S(1)} %pad_maximum_fusion), channel_id=1, replica_groups=mesh['fx'=2,'fz'=8,'fy'=4,'dx'=2,'dc'=2] {'dx'}, use_global_device_ids=true, to_apply=%region_8.9 | all-reduce | flops 32768 | bytes 196608 | tf_op jit(solution)/shard_map/psum | solution.py:198
  338.7 4.8 %all_gather.19 = bf16[128,512]{1,0:T(8,128)(2,1)} all-gather(bf16[128,256]{1,0:T(8,128)(2,1)S(1)} %all-reduce.1), channel_id=1, replica_groups=mesh['fx'=2,'fz'=8,'fy'=4,'dx'=2,'dc'=2] {'dc'}, dimensions={1}, use_global_device_ids=true | all-gather | bytes 196608 | tf_op jit(solution)/shard_map/all_gather | solution.py:199
  343.5 11.1 %all-gather.5.cloned.1.call-done = bf16[8192,512]{1,0:T(8,128)(2,1)} async-done(((bf16[8192,256]{1,0:T(8,128)(2,1)}), bf16[8192,512]{1,0:T(8,128)(2,1)}) %all-gather.5.cloned.1.call-update) | async-done | bytes 8388624 | tf_op jit(solution)/shard_map/all_gather | solution.py:112
  354.6 7.0 %convolution_convert_fusion.7 = bf16[256,512]{1,0:T(8,128)(2,1)S(1)} fusion(bf16[256,8192]{0,1:T(8,128)(2,1)} %bitcast.14, bf16[8192,512]{1,0:T(8,128)(2,1)} %all-gather.5.cloned.1.call-done), kind=kOutput, calls=%fused_computation.29 | convolution fusion | flops 2147614720 | bytes 12845056 | tf_op jit(solution)/shard_map/dot_general | solution.py:115
  362.8 4.2 %all-to-all-start.1 = ((bf16[4,64,512]{2,1,0:T(8,128)(2,1)}), bf16[4,64,512]{2,1,0:T(8,128)(2,1)}, u32[]{:S(2)}, u32[]{:S(2)}) async-start(bf16[4,64,512]{2,1,0:T(8,128)(2,1)} %copy.69), calls=%async_computation.1 | async-start | bytes 524288 | tf_op jit(solution)/shard_map/all_to_all | solution.py:131
  367.0 7.5 %convolution_convert_fusion = bf16[128,8192]{1,0:T(8,128)(2,1)} fusion(bf16[128,512]{1,0:T(8,128)(2,1)S(1)} %bitcast.146, bf16[8192,512]{1,0:T(8,128)(2,1)} %all-gather.5.cloned.1.call-done), kind=kOutput, calls=%fused_computation.2 | convolution fusion | flops 1074790400 | bytes 10616832 | tf_op jit(solution)/shard_map/dot_general | solution.py:169
  380.4 4.6 %reshape_reshape.3 = bf16[1,128,8192]{2,1,0:T(8,128)(2,1)} reshape(bf16[128,2,8,4,128]{4,3,2,1,0:T(4,128)(2,1)} %copy.81) | data formatting | bytes 4194304 | tf_op jit(solution)/shard_map/reshape;reshape | solution.py:203
  394.4 4.8 %all-to-all-start.3 = ((bf16[4,64,512]{2,1,0:T(8,128)(2,1)}), bf16[4,64,512]{2,1,0:T(8,128)(2,1)S(1)}, u32[]{:S(2)}, u32[]{:S(2)}) async-start(bf16[4,64,512]{2,1,0:T(8,128)(2,1)} %copy.83), calls=%async_computation.3 | async-start | bytes 524288 | tf_op jit(solution)/shard_map/all_to_all | solution.py:158
  (108 shorter events, 53.1 us)
Async XLA Ops:
  7.2 15.1 %copy-start = (bf16[1,128,512]{2,1,0:T(8,128)(2,1)S(1)}, bf16[1,128,512]{2,1,0:T(8,128)(2,1)}, u32[]{:S(2)}) copy-start(bf16[1,128,512]{2,1,0:T(8,128)(2,1)} %param.14) | copy-start | bytes 393220
  16.8 10.7 %copy-start.10 = (bf16[1,128,512]{2,1,0:T(8,128)(2,1)S(1)}, bf16[1,128,512]{2,1,0:T(8,128)(2,1)}, u32[]{:S(2)}) copy-start(bf16[1,128,512]{2,1,0:T(8,128)(2,1)} %param.12) | copy-start | bytes 393220
  19.0 8.5 %copy-start.4 = (bf16[1,128,4096]{2,1,0:T(8,128)(2,1)S(1)}, bf16[1,128,4096]{2,1,0:T(8,128)(2,1)}, u32[]{:S(2)}) copy-start(bf16[1,128,4096]{2,1,0:T(8,128)(2,1)} %param.11) | copy-start | bytes 3145732
  19.0 36.5 %collective-permute-start = (bf16[256,8192]{0,1:T(8,128)(2,1)}, bf16[256,8192]{0,1:T(8,128)(2,1)}, u32[]{:S(2)}, u32[]{:S(2)}) collective-permute-start(bf16[256,8192]{0,1:T(8,128)(2,1)} %bitcast.14), channel_id=1, source_target_pairs={{0,1},{1,0},{2,3},{3,2},{4,5},{5,4},{6,7},{7,6},{8,9},{9,8},{10,11... | collective-permute-start | bytes 12582920 | tf_op jit(solution)/shard_map/ppermute | solution.py:114
  23.4 10.7 %all-to-all-start = ((bf16[4,64,512]{2,1,0:T(8,128)(2,1)}), bf16[4,64,512]{2,1,0:T(8,128)(2,1)}, u32[]{:S(2)}, u32[]{:S(2)}) async-start(bf16[4,64,512]{2,1,0:T(8,128)(2,1)} %copy.60), calls=%async_computation | async-start | bytes 524288 | tf_op jit(solution)/shard_map/all_to_all | solution.py:130
  27.5 6.5 %copy-start.14 = (s32[1,2]{1,0:T(1,128)S(1)}, s32[1,2]{1,0:T(1,128)}, u32[]{:S(2)}) copy-start(s32[1,2]{1,0:T(1,128)} %param.18) | copy-start | bytes 28
  27.8 9.9 %copy-start.6 = (bf16[16,8,32,128]{3,2,1,0:T(8,128)(2,1)}, bf16[16,8,32,128]{3,2,1,0:T(8,128)(2,1)S(1)}, u32[]{:S(2)}) copy-start(bf16[16,8,32,128]{3,2,1,0:T(8,128)(2,1)S(1)} %copy.102) | copy-start | bytes 3145732
  28.1 11.6 %copy-start.2 = (bf16[16,8,32,128]{3,2,1,0:T(8,128)(2,1)}, bf16[16,8,32,128]{3,2,1,0:T(8,128)(2,1)S(1)}, u32[]{:S(2)}) copy-start(bf16[16,8,32,128]{3,2,1,0:T(8,128)(2,1)S(1)} %copy.103) | copy-start | bytes 3145732
  42.1 10.9 %all-to-all-start.2 = ((bf16[4,64,512]{2,1,0:T(8,128)(2,1)}), bf16[4,64,512]{2,1,0:T(8,128)(2,1)S(1)}, u32[]{:S(2)}, u32[]{:S(2)}) async-start(bf16[4,64,512]{2,1,0:T(8,128)(2,1)} %copy.78), calls=%async_computation.2 | async-start | bytes 524288 | tf_op jit(solution)/shard_map/all_to_all | solution.py:159
  46.5 72.6 %reduce-scatter.7.cloned.1.call-start = ((), (), s32[]{:S(2)}) async-start(), calls=%async_computation.12 | async-start | bytes 4718592 | tf_op jit(solution)/shard_map/reduce_scatter | solution.py:192
  53.4 2.0 collective-permute-start.1
  64.2 105.5 %reduce-scatter.13.cloned.1.call-start = ((), (), s32[]{:S(2)}) async-start(), calls=%async_computation.15 | async-start | bytes 5242880 | tf_op jit(solution)/shard_map/reduce_scatter | solution.py:193
  68.9 100.9 %copy-start.12 = (bf16[128,512]{1,0:T(8,128)(2,1)S(1)}, bf16[128,512]{1,0:T(8,128)(2,1)}, u32[]{:S(2)}) copy-start(bf16[128,512]{1,0:T(8,128)(2,1)} %param.16) | copy-start | bytes 393220
  68.9 125.0 %reduce-scatter.9.cloned.1.call-start = ((), (), s32[]{:S(2)}) async-start(), calls=%async_computation.13 | async-start | bytes 655360 | tf_op jit(solution)/shard_map/reduce_scatter | solution.py:194
  119.0 113.2 %reduce-scatter.15.cloned.1.call-start = ((), (), s32[]{:S(2)}) async-start(), calls=%async_computation.16 | async-start | bytes 1179648 | tf_op jit(solution)/shard_map/reduce_scatter | solution.py:195
  169.7 122.5 %all-gather.3.cloned.1.call-start = ((), (), s32[]{:S(2)}) async-start(), calls=%async_computation.10 | async-start | bytes 4718592 | tf_op jit(solution)/shard_map/all_gather | solution.py:111
  184.5 123.9 %reduce-scatter.11.cloned.1.call-start = ((), (), s32[]{:S(2)}) async-start(), calls=%async_computation.14 | async-start | bytes 196608 | tf_op jit(solution)/shard_map/reduce_scatter | solution.py:196
  193.9 133.5 %reduce-scatter.17.cloned.1.call-start = ((), (), s32[]{:S(2)}) async-start(), calls=%async_computation.17 | async-start | bytes 196608 | tf_op jit(solution)/shard_map/reduce_scatter | solution.py:197
  232.3 122.3 %all-gather.5.cloned.1.call-start = ((), (), s32[]{:S(2)}) async-start(), calls=%async_computation.11 | async-start | bytes 12582912 | tf_op jit(solution)/shard_map/all_gather | solution.py:112
  362.8 22.2 %all-to-all-start.1 = ((bf16[4,64,512]{2,1,0:T(8,128)(2,1)}), bf16[4,64,512]{2,1,0:T(8,128)(2,1)}, u32[]{:S(2)}, u32[]{:S(2)}) async-start(bf16[4,64,512]{2,1,0:T(8,128)(2,1)} %copy.69), calls=%async_computation.1 | async-start | bytes 524288 | tf_op jit(solution)/shard_map/all_to_all | solution.py:131
  380.4 6.7 %copy-start.3 = (bf16[16,8,32,128]{3,2,1,0:T(8,128)(2,1)S(1)}, bf16[16,8,32,128]{3,2,1,0:T(8,128)(2,1)}, u32[]{:S(2)}) copy-start(bf16[16,8,32,128]{3,2,1,0:T(8,128)(2,1)} %copy-done.2) | copy-start | bytes 3145732
  394.4 11.3 %all-to-all-start.3 = ((bf16[4,64,512]{2,1,0:T(8,128)(2,1)}), bf16[4,64,512]{2,1,0:T(8,128)(2,1)S(1)}, u32[]{:S(2)}, u32[]{:S(2)}) async-start(bf16[4,64,512]{2,1,0:T(8,128)(2,1)} %copy.83), calls=%async_computation.3 | async-start | bytes 524288 | tf_op jit(solution)/shard_map/all_to_all | solution.py:158
  399.7 7.8 %copy-start.1 = (bf16[1,128,512]{2,1,0:T(8,128)(2,1)S(1)}, bf16[1,128,512]{2,1,0:T(8,128)(2,1)}, u32[]{:S(2)}) copy-start(bf16[1,128,512]{2,1,0:T(8,128)(2,1)} %param.14) | copy-start | bytes 393220
  400.4 6.4 %copy-start.9 = (bf16[128,512]{1,0:T(8,128)(2,1)S(1)}, bf16[128,512]{1,0:T(8,128)(2,1)}, u32[]{:S(2)}) copy-start(bf16[128,512]{1,0:T(8,128)(2,1)} %all_gather.19) | copy-start | bytes 393220
  (6 other events, 18.2 us)
Sparse Core Ops, SparseCore 0:
  64.3 54.6 reduce-scatter.6
  121.6 48.0 reduce-scatter.12
  172.2 21.6 reduce-scatter.8
  196.3 35.9 reduce-scatter.14
  233.9 58.2 all-gather.2
  294.5 13.9 reduce-scatter.10
  310.9 16.4 reduce-scatter.16
  329.2 25.3 all-gather.4
where the time goes:
time: 415 us; the launch traced here: 414 us
  waiting for transfers between devices  271 us (65%)
  local copies, waits for them, and re-layouts  37.9 us (9%)
  matrix products  33.7 us (8%)
  blocking collectives  29.9 us (7%)
  starting transfers between devices  22 us (5%)
  between operations  14.6 us (4%)
  other arithmetic  5.17 us (1%)
    all_gather x1, waiting for transfers between devices, per_device(): part = lax.all_gather(part, 'fz', axis=0, tiled=True)  59.8 us
    reduce_scatter x1, waiting for transfers between devices, per_device(): second = lax.psum_scatter(second, 'fy', scatter_dimension=0, tiled=True)  50.6 us
    reduce_scatter x1, waiting for transfers between devices, per_device(): first = lax.psum_scatter(first, 'fz', scatter_dimension=0, tiled=True)  50.1 us
    reduce_scatter x1, waiting for transfers between devices, per_device(): second = lax.psum_scatter(second, 'fz', scatter_dimension=0, tiled=True)  38.3 us
    reduce_scatter x1, waiting for transfers between devices, per_device(): second = lax.psum_scatter(second, 'fx', scatter_dimension=0, tiled=True)  18.9 us
    reduce_scatter x1, waiting for transfers between devices, per_device(): first = lax.psum_scatter(first, 'fx', scatter_dimension=0, tiled=True)  16.3 us
    all_gather x1, waiting for transfers between devices, per_device(): weight_full = lax.all_gather(part, 'dc', axis=1, tiled=True)  11.1 us
    all_gather x1, blocking collectives, per_device(): part = lax.all_gather(part, 'fy', axis=0, tiled=True)  11 us
  transfers between devices with their start and end apart: 14, of which 12 were waited for; matrix products, arithmetic and copies ran while one was open for 9% of the time, Pallas kernels for 0%

commit v1 on v0

--- a/solution.py
+++ b/solution.py
@@ -195,7 +195,9 @@
     second = lax.psum_scatter(second, "fz", scatter_dimension=0, tiled=True)
     first = lax.psum_scatter(first, "fx", scatter_dimension=0, tiled=True)
     second = lax.psum_scatter(second, "fx", scatter_dimension=0, tiled=True)
-    shares = lax.psum(jnp.concatenate([first, second], axis=1), "dx")
+    x = jnp.concatenate([first, second], axis=1)
+    parts = lax.all_gather(x, "dx", axis=0, tiled=False)
+    shares = parts.sum(axis=0)
     grad_weight = lax.all_gather(shares, "dc", axis=1, tiled=True).astype(jnp.bfloat16)
     return (
         grad_query.reshape(1, slot_count * seg_len, -1),

time: 415 us -> 415 us (level)
  blocking collectives: 29.9 us -> 24.7 us
  waiting for transfers between devices: 271 us -> 276 us
    psum x1 -> x0, blocking collectives: 10.4 us -> none  [per_device(): shares = lax.psum(jnp.concatenate([first, second], axis=1), 'dx')]
    all_gather x0 -> x1, blocking collectives: none -> 6.32 us  [per_device(): parts = lax.all_gather(x, 'dx', axis=0, tiled=False)]
    all_gather x1, waiting for transfers between devices: 11.1 us -> 16.3 us  [per_device(): weight_full = lax.all_gather(part, 'dc', axis=1, tiled=True)]
where the time goes in v1:
time: 415 us; the launch traced here: 414 us
  waiting for transfers between devices  276 us (67%)
  local copies, waits for them, and re-layouts  37.9 us (9%)
  matrix products  33.7 us (8%)
  blocking collectives  24.7 us (6%)
  starting transfers between devices  22 us (5%)
  between operations  14.6 us (4%)
  other arithmetic  5.19 us (1%)
    all_gather x1, waiting for transfers between devices, per_device(): part = lax.all_gather(part, 'fz', axis=0, tiled=True)  59.8 us
    reduce_scatter x1, waiting for transfers between devices, per_device(): second = lax.psum_scatter(second, 'fy', scatter_dimension=0, tiled=True)  50.6 us
    reduce_scatter x1, waiting for transfers between devices, per_device(): first = lax.psum_scatter(first, 'fz', scatter_dimension=0, tiled=True)  50.1 us
    reduce_scatter x1, waiting for transfers between devices, per_device(): second = lax.psum_scatter(second, 'fz', scatter_dimension=0, tiled=True)  38.3 us
    reduce_scatter x1, waiting for transfers between devices, per_device(): second = lax.psum_scatter(second, 'fx', scatter_dimension=0, tiled=True)  18.9 us
    all_gather x1, waiting for transfers between devices, per_device(): weight_full = lax.all_gather(part, 'dc', axis=1, tiled=True)  16.3 us
    reduce_scatter x1, waiting for transfers between devices, per_device(): first = lax.psum_scatter(first, 'fx', scatter_dimension=0, tiled=True)  16.3 us
    all_gather x1, blocking collectives, per_device(): part = lax.all_gather(part, 'fy', axis=0, tiled=True)  11 us
  transfers between devices with their start and end apart: 14, of which 12 were waited for; matrix products, arithmetic and copies ran while one was open for 9% of the time, Pallas kernels for 0%

profile of v1, /device:TPU:1, one launch (start us, length us, event | category | flops | bytes accessed | tf_op | source)
XLA Modules:
  0.0 414.3 jit_solution(3784056949232613589)
XLA Ops:
  10.4 4.1 copy.66
  23.4 4.0 all-to-all-start
  28.3 5.8 %all-to-all-done = bf16[4,64,512]{2,1,0:T(8,128)(2,1)} async-done(((bf16[4,64,512]{2,1,0:T(8,128)(2,1)}), bf16[4,64,512]{2,1,0:T(8,128)(2,1)}, u32[]{:S(2)}, u32[]{:S(2)}) %all-to-all-start) | async-done | bytes 262176 | tf_op jit(solution)/shard_map/all_to_all | solution.py:130
  42.1 4.3 %all-to-all-start.2 = ((bf16[4,64,512]{2,1,0:T(8,128)(2,1)}), bf16[4,64,512]{2,1,0:T(8,128)(2,1)S(1)}, u32[]{:S(2)}, u32[]{:S(2)}) async-start(bf16[4,64,512]{2,1,0:T(8,128)(2,1)} %copy.78), calls=%async_computation.2 | async-start | bytes 524288 | tf_op jit(solution)/shard_map/all_to_all | solution.py:159
  46.6 6.4 %all-to-all-done.2 = bf16[4,64,512]{2,1,0:T(8,128)(2,1)S(1)} async-done(((bf16[4,64,512]{2,1,0:T(8,128)(2,1)}), bf16[4,64,512]{2,1,0:T(8,128)(2,1)S(1)}, u32[]{:S(2)}, u32[]{:S(2)}) %all-to-all-start.2) | async-done | bytes 262176 | tf_op jit(solution)/shard_map/all_to_all | solution.py:159
  55.5 4.8 %fusion.2 = f32[8192,256]{1,0:T(8,128)S(1)} fusion(bf16[256,8192]{0,1:T(8,128)(2,1)} %collective-permute-done, bf16[256,8192]{0,1:T(8,128)(2,1)} %bitcast.14, bf16[256,256]{1,0:T(8,128)(2,1)S(1)} %collective-permute-done.1, bf16[256,256]{1,0:T(8,128)(2,1)S(1)} %get-tuple-element.7), kind=kOutput, calls=%fused_computation.3 | convolution fusion | flops 2164785152 | bytes 17039360 | tf_op jit(solution)/shard_map/dot_general | solution.py:184
  60.3 3.9 fusion.68
  64.2 4.6 %copy.87 = f32[4,8,2,128,128]{4,3,2,1,0:T(8,128)} copy(f32[4,8,2,128,128]{4,3,2,0,1:T(8,128)} %bitcast.139) | data formatting | bytes 8388608 | tf_op jit(solution)/shard_map/transpose | solution.py:190
  68.9 50.1 %reduce-scatter.7.cloned.1.call-done = f32[1024,128]{1,0:T(8,128)} async-done(((f32[8192,128]{1,0:T(8,128)}), f32[1024,128]{1,0:T(8,128)}) %reduce-scatter.7.cloned.1.call-update) | async-done | bytes 524304 | tf_op jit(solution)/shard_map/reduce_scatter | solution.py:192
  119.1 50.6 %reduce-scatter.13.cloned.1.call-done = f32[2048,128]{1,0:T(8,128)} async-done(((f32[8192,128]{1,0:T(8,128)}), f32[2048,128]{1,0:T(8,128)}) %reduce-scatter.13.cloned.1.call-update) | async-done | bytes 1048592 | tf_op jit(solution)/shard_map/reduce_scatter | solution.py:193
  169.7 3.8 all_gather.21
  173.5 11.0 %all_gather.22 = bf16[1024,256]{1,0:T(8,128)(2,1)} all-gather(bf16[256,256]{1,0:T(8,128)(2,1)S(1)} %all_gather.21), channel_id=1, replica_groups=mesh['fx'=2,'fz'=8,'fy'=4,'dx'=2,'dc'=2] {'fy'}, dimensions={0}, use_global_device_ids=true | all-gather | bytes 655360 | tf_op jit(solution)/shard_map/all_gather | solution.py:110
  184.6 9.3 %reduce-scatter.9.cloned.1.call-done = f32[256,128]{1,0:T(8,128)} async-done(((f32[1024,128]{1,0:T(8,128)}), f32[256,128]{1,0:T(8,128)}) %reduce-scatter.9.cloned.1.call-update) | async-done | bytes 131088 | tf_op jit(solution)/shard_map/reduce_scatter | solution.py:194
  193.9 38.3 %reduce-scatter.15.cloned.1.call-done = f32[256,128]{1,0:T(8,128)} async-done(((f32[2048,128]{1,0:T(8,128)}), f32[256,128]{1,0:T(8,128)}) %reduce-scatter.15.cloned.1.call-update) | async-done | bytes 131088 | tf_op jit(solution)/shard_map/reduce_scatter | solution.py:195
  232.3 59.8 %all-gather.4.cloned.1.call-done = bf16[8192,256]{1,0:T(8,128)(2,1)} async-done(((bf16[1024,256]{1,0:T(8,128)(2,1)}), bf16[8192,256]{1,0:T(8,128)(2,1)}) %all-gather.4.cloned.1.call-update) | async-done | bytes 4194320 | tf_op jit(solution)/shard_map/all_gather | solution.py:111
  292.2 16.3 %reduce-scatter.11.cloned.1.call-done = f32[128,128]{1,0:T(8,128)} async-done(((f32[256,128]{1,0:T(8,128)}), f32[128,128]{1,0:T(8,128)}) %reduce-scatter.11.cloned.1.call-update) | async-done | bytes 65552 | tf_op jit(solution)/shard_map/reduce_scatter | solution.py:196
  308.5 18.9 %reduce-scatter.17.cloned.1.call-done = f32[128,128]{1,0:T(8,128)} async-done(((f32[256,128]{1,0:T(8,128)}), f32[128,128]{1,0:T(8,128)}) %reduce-scatter.17.cloned.1.call-update) | async-done | bytes 65552 | tf_op jit(solution)/shard_map/reduce_scatter | solution.py:197
  328.3 6.3 %all-gather = f32[256,256]{1,0:T(8,128)S(1)} all-gather(f32[128,256]{1,0:T(8,128)S(1)} %pad_maximum_fusion), channel_id=2, replica_groups=mesh['fx'=2,'fz'=8,'fy'=4,'dx'=2,'dc'=2] {'dx'}, dimensions={0}, use_global_device_ids=true | all-gather | bytes 393216 | tf_op jit(solution)/shard_map/all_gather | solution.py:199
  338.2 16.3 %all-gather.6.cloned.1.call-done = bf16[8192,512]{1,0:T(8,128)(2,1)} async-done(((bf16[8192,256]{1,0:T(8,128)(2,1)}), bf16[8192,512]{1,0:T(8,128)(2,1)}) %all-gather.6.cloned.1.call-update) | async-done | bytes 8388624 | tf_op jit(solution)/shard_map/all_gather | solution.py:112
  354.6 7.0 %convolution_convert_fusion.7 = bf16[256,512]{1,0:T(8,128)(2,1)S(1)} fusion(bf16[256,8192]{0,1:T(8,128)(2,1)} %bitcast.14, bf16[8192,512]{1,0:T(8,128)(2,1)} %all-gather.6.cloned.1.call-done), kind=kOutput, calls=%fused_computation.29 | convolution fusion | flops 2147614720 | bytes 12845056 | tf_op jit(solution)/shard_map/dot_general | solution.py:115
  362.8 4.2 %all-to-all-start.1 = ((bf16[4,64,512]{2,1,0:T(8,128)(2,1)}), bf16[4,64,512]{2,1,0:T(8,128)(2,1)}, u32[]{:S(2)}, u32[]{:S(2)}) async-start(bf16[4,64,512]{2,1,0:T(8,128)(2,1)} %copy.69), calls=%async_computation.1 | async-start | bytes 524288 | tf_op jit(solution)/shard_map/all_to_all | solution.py:131
  367.0 7.5 %convolution_convert_fusion = bf16[128,8192]{1,0:T(8,128)(2,1)} fusion(bf16[128,512]{1,0:T(8,128)(2,1)S(1)} %bitcast.147, bf16[8192,512]{1,0:T(8,128)(2,1)} %all-gather.6.cloned.1.call-done), kind=kOutput, calls=%fused_computation.2 | convolution fusion | flops 1074790400 | bytes 10616832 | tf_op jit(solution)/shard_map/dot_general | solution.py:169
  380.4 4.6 %reshape_reshape.3 = bf16[1,128,8192]{2,1,0:T(8,128)(2,1)} reshape(bf16[128,2,8,4,128]{4,3,2,1,0:T(4,128)(2,1)} %copy.81) | data formatting | bytes 4194304 | tf_op jit(solution)/shard_map/reshape;reshape | solution.py:205
  394.4 4.8 %all-to-all-start.3 = ((bf16[4,64,512]{2,1,0:T(8,128)(2,1)}), bf16[4,64,512]{2,1,0:T(8,128)(2,1)S(1)}, u32[]{:S(2)}, u32[]{:S(2)}) async-start(bf16[4,64,512]{2,1,0:T(8,128)(2,1)} %copy.83), calls=%async_computation.3 | async-start | bytes 524288 | tf_op jit(solution)/shard_map/all_to_all | solution.py:158
  (109 shorter events, 52.9 us)
Async XLA Ops:
  7.2 15.1 %copy-start = (bf16[1,128,512]{2,1,0:T(8,128)(2,1)S(1)}, bf16[1,128,512]{2,1,0:T(8,128)(2,1)}, u32[]{:S(2)}) copy-start(bf16[1,128,512]{2,1,0:T(8,128)(2,1)} %param.14) | copy-start | bytes 393220
  16.8 10.7 %copy-start.10 = (bf16[1,128,512]{2,1,0:T(8,128)(2,1)S(1)}, bf16[1,128,512]{2,1,0:T(8,128)(2,1)}, u32[]{:S(2)}) copy-start(bf16[1,128,512]{2,1,0:T(8,128)(2,1)} %param.12) | copy-start | bytes 393220
  19.0 8.5 %copy-start.4 = (bf16[1,128,4096]{2,1,0:T(8,128)(2,1)S(1)}, bf16[1,128,4096]{2,1,0:T(8,128)(2,1)}, u32[]{:S(2)}) copy-start(bf16[1,128,4096]{2,1,0:T(8,128)(2,1)} %param.11) | copy-start | bytes 3145732
  19.0 36.5 %collective-permute-start = (bf16[256,8192]{0,1:T(8,128)(2,1)}, bf16[256,8192]{0,1:T(8,128)(2,1)}, u32[]{:S(2)}, u32[]{:S(2)}) collective-permute-start(bf16[256,8192]{0,1:T(8,128)(2,1)} %bitcast.14), channel_id=1, source_target_pairs={{0,1},{1,0},{2,3},{3,2},{4,5},{5,4},{6,7},{7,6},{8,9},{9,8},{10,11... | collective-permute-start | bytes 12582920 | tf_op jit(solution)/shard_map/ppermute | solution.py:114
  23.4 10.7 %all-to-all-start = ((bf16[4,64,512]{2,1,0:T(8,128)(2,1)}), bf16[4,64,512]{2,1,0:T(8,128)(2,1)}, u32[]{:S(2)}, u32[]{:S(2)}) async-start(bf16[4,64,512]{2,1,0:T(8,128)(2,1)} %copy.60), calls=%async_computation | async-start | bytes 524288 | tf_op jit(solution)/shard_map/all_to_all | solution.py:130
  27.5 6.5 %copy-start.14 = (s32[1,2]{1,0:T(1,128)S(1)}, s32[1,2]{1,0:T(1,128)}, u32[]{:S(2)}) copy-start(s32[1,2]{1,0:T(1,128)} %param.18) | copy-start | bytes 28
  27.8 9.9 %copy-start.6 = (bf16[16,8,32,128]{3,2,1,0:T(8,128)(2,1)}, bf16[16,8,32,128]{3,2,1,0:T(8,128)(2,1)S(1)}, u32[]{:S(2)}) copy-start(bf16[16,8,32,128]{3,2,1,0:T(8,128)(2,1)S(1)} %copy.102) | copy-start | bytes 3145732
  28.1 11.6 %copy-start.2 = (bf16[16,8,32,128]{3,2,1,0:T(8,128)(2,1)}, bf16[16,8,32,128]{3,2,1,0:T(8,128)(2,1)S(1)}, u32[]{:S(2)}) copy-start(bf16[16,8,32,128]{3,2,1,0:T(8,128)(2,1)S(1)} %copy.103) | copy-start | bytes 3145732
  42.1 10.9 %all-to-all-start.2 = ((bf16[4,64,512]{2,1,0:T(8,128)(2,1)}), bf16[4,64,512]{2,1,0:T(8,128)(2,1)S(1)}, u32[]{:S(2)}, u32[]{:S(2)}) async-start(bf16[4,64,512]{2,1,0:T(8,128)(2,1)} %copy.78), calls=%async_computation.2 | async-start | bytes 524288 | tf_op jit(solution)/shard_map/all_to_all | solution.py:159
  46.5 72.6 %reduce-scatter.7.cloned.1.call-start = ((), (), s32[]{:S(2)}) async-start(), calls=%async_computation.12 | async-start | bytes 4718592 | tf_op jit(solution)/shard_map/reduce_scatter | solution.py:192
  53.4 2.0 collective-permute-start.1
  64.2 105.5 %reduce-scatter.13.cloned.1.call-start = ((), (), s32[]{:S(2)}) async-start(), calls=%async_computation.15 | async-start | bytes 5242880 | tf_op jit(solution)/shard_map/reduce_scatter | solution.py:193
  68.9 100.9 %copy-start.12 = (bf16[128,512]{1,0:T(8,128)(2,1)S(1)}, bf16[128,512]{1,0:T(8,128)(2,1)}, u32[]{:S(2)}) copy-start(bf16[128,512]{1,0:T(8,128)(2,1)} %param.16) | copy-start | bytes 393220
  68.9 125.0 %reduce-scatter.9.cloned.1.call-start = ((), (), s32[]{:S(2)}) async-start(), calls=%async_computation.13 | async-start | bytes 655360 | tf_op jit(solution)/shard_map/reduce_scatter | solution.py:194
  119.0 113.2 %reduce-scatter.15.cloned.1.call-start = ((), (), s32[]{:S(2)}) async-start(), calls=%async_computation.16 | async-start | bytes 1179648 | tf_op jit(solution)/shard_map/reduce_scatter | solution.py:195
  169.7 122.5 %all-gather.4.cloned.1.call-start = ((), (), s32[]{:S(2)}) async-start(), calls=%async_computation.10 | async-start | bytes 4718592 | tf_op jit(solution)/shard_map/all_gather | solution.py:111
  184.5 123.9 %reduce-scatter.11.cloned.1.call-start = ((), (), s32[]{:S(2)}) async-start(), calls=%async_computation.14 | async-start | bytes 196608 | tf_op jit(solution)/shard_map/reduce_scatter | solution.py:196
  193.9 133.5 %reduce-scatter.17.cloned.1.call-start = ((), (), s32[]{:S(2)}) async-start(), calls=%async_computation.17 | async-start | bytes 196608 | tf_op jit(solution)/shard_map/reduce_scatter | solution.py:197
  232.3 122.3 %all-gather.6.cloned.1.call-start = ((), (), s32[]{:S(2)}) async-start(), calls=%async_computation.11 | async-start | bytes 12582912 | tf_op jit(solution)/shard_map/all_gather | solution.py:112
  362.8 22.2 %all-to-all-start.1 = ((bf16[4,64,512]{2,1,0:T(8,128)(2,1)}), bf16[4,64,512]{2,1,0:T(8,128)(2,1)}, u32[]{:S(2)}, u32[]{:S(2)}) async-start(bf16[4,64,512]{2,1,0:T(8,128)(2,1)} %copy.69), calls=%async_computation.1 | async-start | bytes 524288 | tf_op jit(solution)/shard_map/all_to_all | solution.py:131
  380.4 6.7 %copy-start.3 = (bf16[16,8,32,128]{3,2,1,0:T(8,128)(2,1)S(1)}, bf16[16,8,32,128]{3,2,1,0:T(8,128)(2,1)}, u32[]{:S(2)}) copy-start(bf16[16,8,32,128]{3,2,1,0:T(8,128)(2,1)} %copy-done.2) | copy-start | bytes 3145732
  394.4 11.3 %all-to-all-start.3 = ((bf16[4,64,512]{2,1,0:T(8,128)(2,1)}), bf16[4,64,512]{2,1,0:T(8,128)(2,1)S(1)}, u32[]{:S(2)}, u32[]{:S(2)}) async-start(bf16[4,64,512]{2,1,0:T(8,128)(2,1)} %copy.83), calls=%async_computation.3 | async-start | bytes 524288 | tf_op jit(solution)/shard_map/all_to_all | solution.py:158
  399.7 7.8 %copy-start.1 = (bf16[1,128,512]{2,1,0:T(8,128)(2,1)S(1)}, bf16[1,128,512]{2,1,0:T(8,128)(2,1)}, u32[]{:S(2)}) copy-start(bf16[1,128,512]{2,1,0:T(8,128)(2,1)} %param.14) | copy-start | bytes 393220
  400.4 6.4 %copy-start.9 = (bf16[128,512]{1,0:T(8,128)(2,1)S(1)}, bf16[128,512]{1,0:T(8,128)(2,1)}, u32[]{:S(2)}) copy-start(bf16[128,512]{1,0:T(8,128)(2,1)} %all_gather.27) | copy-start | bytes 393220
  (6 other events, 18.2 us)
Sparse Core Ops, SparseCore 0:
  64.3 54.6 reduce-scatter.6
  121.6 48.0 reduce-scatter.12
  172.2 21.6 reduce-scatter.8
  196.3 35.9 reduce-scatter.14
  233.9 58.2 all-gather.3
  294.5 13.9 reduce-scatter.10
  310.9 16.4 reduce-scatter.16
  329.2 25.3 all-gather.5
